TPU v7x, 128 devices: a whole 4x4x4 slice. The times are simulated.
128 devices in a mesh: seq: 16 (over y, x_lo, core), tp: 8 (over z, x_hi).
Axes of the slice: x: 4 (x_hi: 2, x_lo: 2; x = x_hi * 2 + x_lo), y: 4, z: 4, core: 2. Of those that a mesh axis runs over, the one named last changes fastest.
Arguments:
- tokens: bfloat16 [8192, 4096], P('seq'), may hold values from -6 to 6
- norm_gain: bfloat16 [4096], replicated, may hold values from 0.099609375 to 1.8984375
- w_query: bfloat16 [4096, 4096], P(None, 'tp'), may hold values from -4 to 4
- w_key: bfloat16 [4096, 512], replicated, may hold values from -1 to 1
- w_value: bfloat16 [4096, 512], replicated, may hold values from -0.09375 to 0.09375
- w_out: bfloat16 [4096, 4096], P('tp'), may hold values from -0.375 to 0.375
- prompt_lengths: int32 [16], replicated, may hold values from 1 to 6144, 8192 in all
- page_slots: int32 [64], replicated, may hold values from 0 to 63, each once
Outputs:
- attended: bfloat16 [8192, 4096], P(('seq', 'tp'))
- kv_cache: bfloat16 [64, 128, 1024], P('seq', None, 'tp')
Inputs may be any that keep to these rules, and one draw needn't show every extreme that they name: `prompt_lengths`: the lengths sum to 8192; the longest prompt has exactly 6144 tokens. `page_slots`: every value appears exactly once.
All inputs are finite; a program needn't handle non-finite values.
Results may differ from a plain program's by a relative error of at most 0.015.
Values may be sent and summed in bfloat16 or wider, within the bound.
No kernel may reach another device: no remote copies, remote signals or barrier semaphores. Data moves between devices by JAX's collectives and lax.ppermute only.
A program may use at most 128 MiB of HBM per device.

v0:
```python
import functools

import jax
import jax.numpy as jnp
from jax import lax
from jax.experimental import pallas as pl
from jax.experimental.pallas import tpu as pltpu
from jax.sharding import PartitionSpec as P

HD = 128
PAGE = 128
BQ = 256
CHUNKS = 2
BK = 1024


epsilon = 1e-05
rope_base = 5000000.0


def segment_start(token_index, prompt_lengths):
    prompt_ends = jnp.cumsum(prompt_lengths)
    finished = prompt_ends[None, :] <= token_index[:, None]
    return jnp.sum(jnp.where(finished, prompt_lengths[None, :], 0), axis=1)


def rotate(vectors, position):
    half_size = HD // 2
    frequency = rope_base ** (-(2.0 * jnp.arange(half_size, dtype=jnp.float32)) / HD)
    angle = position.astype(jnp.float32)[:, None] * frequency[None, :]
    cosine = jnp.cos(angle)[:, None, :]
    sine = jnp.sin(angle)[:, None, :]
    first_half = vectors[..., :half_size]
    second_half = vectors[..., half_size:]
    return jnp.concatenate(
        [first_half * cosine - second_half * sine, second_half * cosine + first_half * sine],
        axis=-1,
    )


def normalize(tokens, norm_gain):
    hidden = tokens.astype(jnp.float32)
    factor = lax.rsqrt(jnp.mean(hidden * hidden, axis=-1, keepdims=True) + epsilon)
    return (hidden * factor * norm_gain.astype(jnp.float32)).astype(jnp.bfloat16)


def flash_kernel(lo_ref, hi_ref, base_ref, last_start_ref, q_ref, start_ref, index_ref, kv_ref, o_ref):
    i = pl.program_id(0)
    heads = q_ref.shape[1] // HD
    row_index = index_ref[...]
    row_start = start_ref[...]
    scale = HD ** (-0.5)

    def step(kb, carry, masked):
        offset = pl.multiple_of(kb * BK, BK)
        keys = kv_ref[pl.ds(offset, BK), pl.ds(0, HD)]
        values = kv_ref[pl.ds(offset, BK), pl.ds(HD, HD)]
        values_ones = jnp.concatenate([values, jnp.ones((BK, HD), values.dtype)], axis=1)
        if masked:
            key_index = offset + lax.broadcasted_iota(jnp.int32, (1, BK), 1)
            visible = (key_index >= row_start) & (key_index <= row_index)
        updated = []
        for h in range(heads):
            running_max, running_sum, weighted = carry[h]
            q = q_ref[:, pl.ds(h * HD, HD)]
            scores = lax.dot_general(
                q, keys, (((1,), (1,)), ((), ())), preferred_element_type=jnp.float32
            ) * scale
            if masked:
                scores = jnp.where(visible, scores, -1e30)
            fresh_max = jnp.maximum(running_max, jnp.max(scores, axis=1, keepdims=True))
            weights = jnp.exp(scores - fresh_max)
            if masked:
                weights = jnp.where(visible, weights, 0.0)
            shrink = jnp.exp(running_max - fresh_max)
            both = jnp.dot(
                weights.astype(jnp.bfloat16), values_ones, preferred_element_type=jnp.float32
            )
            running_sum = running_sum * shrink + both[:, HD:]
            weighted = weighted * shrink + both[:, :HD]
            updated.append((fresh_max, running_sum, weighted))
        return tuple(updated)

    lo = lo_ref[i]
    hi = hi_ref[i] + 1
    full_lo = (last_start_ref[i] + BK - 1) // BK
    full_hi = (base_ref[i] + 1) // BK
    mid_lo = jnp.minimum(jnp.maximum(full_lo, lo), hi)
    mid_hi = jnp.maximum(mid_lo, jnp.minimum(full_hi, hi))
    carry = tuple(
        (
            jnp.full((BQ, 1), -1e30, jnp.float32),
            jnp.zeros((BQ, HD), jnp.float32),
            jnp.zeros((BQ, HD), jnp.float32),
        )
        for h in range(heads)
    )
    before = mid_lo - lo

    def masked_step(j, carry):
        kb = jnp.where(j < before, lo + j, mid_hi + j - before)
        return step(kb, carry, masked=True)

    carry = lax.fori_loop(0, before + hi - mid_hi, masked_step, carry)
    carry = lax.fori_loop(mid_lo, mid_hi, functools.partial(step, masked=False), carry)
    for h in range(heads):
        running_max, running_sum, weighted = carry[h]
        o_ref[:, pl.ds(h * HD, HD)] = (weighted / running_sum).astype(o_ref.dtype)


def flash_attention(queries, row_start, row_index, key_values, bounds):
    rows, width = queries.shape
    q_blocks = rows // BQ
    kv_rows = key_values.shape[0]
    rows_of = lambda i, *_: (i, 0)
    grid_spec = pltpu.PrefetchScalarGridSpec(
        num_scalar_prefetch=4,
        grid=(q_blocks,),
        in_specs=[
            pl.BlockSpec((BQ, width), rows_of),
            pl.BlockSpec((BQ, 1), rows_of),
            pl.BlockSpec((BQ, 1), rows_of),
            pl.BlockSpec((kv_rows, 2 * HD), lambda i, *_: (0, 0)),
        ],
        out_specs=pl.BlockSpec((BQ, width), rows_of),
    )
    return pl.pallas_call(
        flash_kernel,
        grid_spec=grid_spec,
        out_shape=jax.ShapeDtypeStruct((rows, width), jnp.bfloat16),
    )(*bounds, queries, row_start, row_index, key_values)


def on_device(tokens, norm_gain, w_query, w_key, w_value, w_out, prompt_lengths, page_slots):
    row_count = tokens.shape[0]
    tp_count = lax.axis_size("tpz") * lax.axis_size("tpx")
    seq_rank = lax.axis_index("seq")
    tp_rank = lax.axis_index("tpz") * lax.axis_size("tpx") + lax.axis_index("tpx")
    heads_here = w_query.shape[1] // HD
    kv_heads = w_key.shape[1] // HD
    sharing = tp_count // kv_heads
    kv_head = tp_rank // sharing
    token_index = seq_rank * row_count + jnp.arange(row_count, dtype=jnp.int32)
    start = segment_start(token_index, prompt_lengths)
    position = token_index - start
    normed = normalize(tokens, norm_gain)

    key_columns = lax.dynamic_slice_in_dim(w_key, kv_head * HD, HD, 1)
    value_columns = lax.dynamic_slice_in_dim(w_value, kv_head * HD, HD, 1)
    keys_here = rotate(
        jnp.dot(normed, key_columns, preferred_element_type=jnp.float32)[:, None, :], position
    )[:, 0].astype(jnp.bfloat16)
    values_here = jnp.dot(normed, value_columns, preferred_element_type=jnp.float32).astype(
        jnp.bfloat16
    )
    keys_values = jnp.concatenate([keys_here, values_here], axis=1)
    gathered = lax.all_gather(keys_values, "seq", axis=0, tiled=True)

    queries = rotate(
        jnp.dot(normed, w_query, preferred_element_type=jnp.float32).reshape(
            row_count, heads_here, HD
        ),
        position,
    ).astype(jnp.bfloat16).reshape(row_count, heads_here * HD)

    piece = row_count // tp_count // CHUNKS
    chunk_queries = queries.reshape(tp_count, CHUNKS, piece, heads_here * HD)
    chunk_start = start.reshape(tp_count, CHUNKS, piece)
    chunk_index = token_index.reshape(tp_count, CHUNKS, piece)
    chunk_inputs = []
    for c in range(CHUNKS):
        q_rows = chunk_queries[:, c].reshape(tp_count * piece, heads_here * HD)
        s_rows = chunk_start[:, c].reshape(tp_count * piece)
        i_rows = chunk_index[:, c].reshape(tp_count * piece)
        bounds = (s_rows[:1] // BK, i_rows[-1:] // BK, i_rows[:1], s_rows[-1:])
        chunk_inputs.append((q_rows, s_rows[:, None], i_rows[:, None], bounds))
    chunk_inputs = lax.optimization_barrier(chunk_inputs)
    outputs = []
    for q_rows, s_rows, i_rows, bounds in chunk_inputs:
        heads_out = flash_attention(q_rows, s_rows, i_rows, gathered, bounds)
        partial_out = jnp.dot(heads_out, w_out, preferred_element_type=jnp.float32).astype(
            jnp.bfloat16
        )
        received = lax.all_to_all(
            partial_out, ("tpz", "tpx"), split_axis=0, concat_axis=0, tiled=True
        ).reshape(tp_count, piece, -1)
        summed = received[0].astype(jnp.float32)
        for t in range(1, tp_count):
            summed = summed + received[t].astype(jnp.float32)
        outputs.append(summed.astype(jnp.bfloat16))
    attended = jnp.stack(outputs, axis=0).reshape(-1, outputs[0].shape[1])

    cache_width = 2 * HD // sharing
    cache_column = tp_rank % sharing * cache_width
    slots_here = row_count // PAGE
    page_total = page_slots.shape[0]
    wanted = seq_rank * slots_here + jnp.arange(slots_here, dtype=jnp.int32)
    page_of_slot = jnp.sum(
        jnp.where(
            page_slots[None, :] == wanted[:, None],
            jnp.arange(page_total, dtype=jnp.int32)[None, :],
            0,
        ),
        axis=1,
    )
    pages = [
        lax.dynamic_slice(gathered, (page_of_slot[j] * PAGE, cache_column), (PAGE, cache_width))
        for j in range(slots_here)
    ]
    cache_here = jnp.stack(pages, axis=0)
    return (attended, cache_here)


def solution(mesh):
    seq_size, tp_size = mesh.devices.shape
    split_mesh = jax.sharding.Mesh(
        mesh.devices.reshape(seq_size, tp_size // 2, 2), ("seq", "tpz", "tpx")
    )
    tp = ("tpz", "tpx")
    placed = (P("seq", None), P(), P(None, tp), P(), P(), P(tp, None), P(), P())
    return jax.shard_map(
        on_device,
        mesh=split_mesh,
        in_specs=placed,
        out_specs=(P(("seq",) + tp, None), P("seq", None, tp)),
        check_vma=False,
    )
```

profile of v0, /device:TPU:24, one launch (start us, length us, event | category | flops | bytes accessed | tf_op | source)
XLA Modules:
  0.0 157.9 jit_solution(8826749004438801124)
XLA Ops:
  7.3 3.1 %fusion = f32[512]{0:T(512)S(1)} fusion(bf16[512,4096]{1,0:T(8,128)(2,1)} %param.8), kind=kLoop, calls=%fused_computation.2 | loop fusion | flops 6290944 | bytes 4196352 | tf_op jit(solution)/shard_map/reduce_sum | solution.py:43
  10.4 0.1 copy.32
  10.5 0.1 reduce
  10.6 0.1 select_reduce_fusion
  10.8 3.9 %convolution_convert_fusion.2 = bf16[512,128]{1,0:T(8,128)(2,1)S(1)} fusion(bf16[4096,512]{1,0:T(8,128)(2,1)} %param.12, s32[]{:T(128)S(6)} %select_n.61, bf16[512,4096]{1,0:T(8,128)(2,1)} %param.8, f32[4096]{0:T(1024)S(1)} %convert_element_type.108, f32[512]{0:T(512)S(1)} %add_rsqrt_fusion), kind=kOutput, calls=%fused_computation.8 | convolution fusion | flops 545325056 | bytes 5392388 | tf_op jit(solution)/shard_map/dot_general | solution.py:153
  14.7 2.5 %convolution_bitcast_fusion = f32[512,1,128]{2,0,1:T(8,128)S(1)} fusion(bf16[4096,512]{1,0:T(8,128)(2,1)} %param.11, s32[]{:T(128)S(6)} %select_n.61, bf16[512,4096]{1,0:T(8,128)(2,1)S(1)} %copy-done, f32[4096]{0:T(1024)S(1)} %convert_element_type.108, f32[512]{0:T(512)S(1)} %add_rsqrt_fusion), kind=kOutput, calls=%fused_computation.7 | convolution fusion | flops 545259520 | bytes 5523460 | tf_op jit(solution)/shard_map/dot_general | solution.py:151
  17.3 1.2 fusion.10
  18.5 0.1 maximum_bitcast_fusion
  18.6 0.7 pad_maximum_fusion.2
  19.4 0.1 reshape.280
  19.5 0.1 reshape_squeeze.23
  19.6 0.1 broadcast_in_dim_reshape_squeeze.15
  19.6 0.1 reshape_squeeze.20
  19.7 0.1 broadcast_in_dim_reshape_squeeze.13
  19.8 0.1 reshape_squeeze.22
  19.9 0.6 fusion.22
  25.7 0.1 reshape_squeeze.19
  25.8 0.6 fusion.24
  31.6 0.1 broadcast_in_dim_reshape_squeeze.14
  31.7 6.0 %fusion.17 = f32[512,512]{0,1:T(8,128)S(1)} fusion(bf16[4096,512]{1,0:T(8,128)(2,1)} %param.10, bf16[512,4096]{1,0:T(8,128)(2,1)} %param.8, f32[4096]{0:T(1024)S(1)} %convert_element_type.108, f32[512]{0:T(512)S(1)} %add_rsqrt_fusion), kind=kOutput, calls=%fused_computation.48 | convolution fusion | flops 2155872256 | bytes 9455616 | tf_op jit(solution)/shard_map/dot_general | solution.py:160
  37.7 0.1 fusion.19
  37.8 0.4 copy.44
  38.2 0.4 copy.43
  38.6 1.0 multiply_cosine_fusion.1
  39.6 0.6 subtract_convert_fusion
  40.2 0.7 pad_maximum_fusion
  40.9 0.2 convert_element_type.111
  41.2 0.8 fusion.20
  42.0 0.8 copy.39.start_ref
  42.8 0.8 copy.40.index_ref
  43.6 14.4 %all-gather.2.cloned.1.call-done.kv_ref = bf16[8192,256]{1,0:T(8,128)(2,1)} async-done(((bf16[512,256]{1,0:T(8,128)(2,1)}), bf16[8192,256]{1,0:T(8,128)(2,1)}) %all-gather.2.cloned.1.call-update) | async-done | bytes 4194320 | tf_op jit(solution)/shard_map/all_gather | solution.py:157
  58.0 17.7 %shard_map.96 = bf16[256,512]{1,0:T(8,128)(2,1)} custom-call(s32[1]{0:T(128)S(6)} %select_n.58.lo_ref, s32[1]{0:T(128)S(6)} %select_n.59.hi_ref, s32[1]{0:T(128)} %get-tuple-element.25.base_ref, s32[1]{0:T(128)} %get-tuple-element.26.last_start_ref, bf16[256,512]{1,0:T(8,128)(2,1)} %bitcast.42, s32[256,1]{1,0:T(8,128)} %copy.39.start_ref, ...), custom_call_target="tpu_custom_call" | custom-call | tf_op jit(solution)/shard_map/pallas_call | solution.py:127
  75.8 4.9 %convolution_convert_fusion = bf16[256,4096]{1,0:T(8,128)(2,1)} fusion(bf16[256,512]{1,0:T(8,128)(2,1)} %shard_map.96, bf16[512,4096]{1,0:T(8,128)(2,1)} %param.13), kind=kOutput, calls=%fused_computation.5 | convolution fusion | flops 1074790400 | bytes 6553600 | tf_op jit(solution)/shard_map/dot_general | solution.py:181
  80.6 6.6 %all-to-all-start.1 = ((bf16[8,32,4096]{2,1,0:T(8,128)(2,1)}), bf16[8,32,4096]{2,1,0:T(8,128)(2,1)S(1)}, u32[]{:S(2)}, u32[]{:S(2)}) async-start(bf16[8,32,4096]{2,1,0:T(8,128)(2,1)} %bitcast.39), calls=%async_computation.1 | async-start | bytes 4194304 | tf_op jit(solution)/shard_map/all_to_all | solution.py:184
  87.2 0.8 copy.37.start_ref
  88.0 0.8 copy.38.index_ref
  88.8 17.6 %shard_map.95 = bf16[256,512]{1,0:T(8,128)(2,1)} custom-call(s32[1]{0:T(128)S(6)} %select_n.56.lo_ref, s32[1]{0:T(128)S(6)} %select_n.57.hi_ref, s32[1]{0:T(128)} %get-tuple-element.18.base_ref, s32[1]{0:T(128)} %get-tuple-element.19.last_start_ref, bf16[256,512]{1,0:T(8,128)(2,1)} %bitcast.41, s32[256,1]{1,0:T(8,128)} %copy.37.start_ref, ...), custom_call_target="tpu_custom_call" | custom-call | tf_op jit(solution)/shard_map/pallas_call | solution.py:127
  106.4 4.9 %convolution_convert_fusion.1 = bf16[256,4096]{1,0:T(8,128)(2,1)} fusion(bf16[256,512]{1,0:T(8,128)(2,1)} %shard_map.95, bf16[512,4096]{1,0:T(8,128)(2,1)} %param.13), kind=kOutput, calls=%fused_computation.6 | convolution fusion | flops 1074790400 | bytes 6553600 | tf_op jit(solution)/shard_map/dot_general | solution.py:181
  111.2 4.9 %all-to-all-done.1 = bf16[8,32,4096]{2,1,0:T(8,128)(2,1)S(1)} async-done(((bf16[8,32,4096]{2,1,0:T(8,128)(2,1)}), bf16[8,32,4096]{2,1,0:T(8,128)(2,1)S(1)}, u32[]{:S(2)}, u32[]{:S(2)}) %all-to-all-start.1) | async-done | bytes 2097184 | tf_op jit(solution)/shard_map/all_to_all | solution.py:184
  116.1 4.4 %all-to-all-start = ((bf16[8,32,4096]{2,1,0:T(8,128)(2,1)}), bf16[8,32,4096]{2,1,0:T(8,128)(2,1)}, u32[]{:S(2)}, u32[]{:S(2)}) async-start(bf16[8,32,4096]{2,1,0:T(8,128)(2,1)} %bitcast.38), calls=%async_computation | async-start | bytes 4194304 | tf_op jit(solution)/shard_map/all_to_all | solution.py:184
  120.5 0.2 select_reduce_fusion.1
  120.7 0.6 fusion.26
  123.7 0.8 dynamic-slice_bitcast_fusion.3
  124.6 0.7 pad_maximum_fusion.3
  125.2 0.3 add_convert_fusion.1
  125.5 23.0 %all-to-all-done = bf16[8,32,4096]{2,1,0:T(8,128)(2,1)} async-done(((bf16[8,32,4096]{2,1,0:T(8,128)(2,1)}), bf16[8,32,4096]{2,1,0:T(8,128)(2,1)}, u32[]{:S(2)}, u32[]{:S(2)}) %all-to-all-start) | async-done | bytes 2097184 | tf_op jit(solution)/shard_map/all_to_all | solution.py:184
  148.5 1.8 %add_convert_fusion.2 = bf16[1,32,4096]{2,1,0:T(8,128)(2,1)S(1)} fusion(bf16[8,32,4096]{2,1,0:T(8,128)(2,1)} %all-to-all-done), kind=kLoop, calls=%fused_computation.16 | loop fusion | flops 2097152 | bytes 2359296 | tf_op jit(solution)/shard_map/convert_element_type | solution.py:190
  150.2 0.8 pad_maximum_fusion.1
  (21 shorter events, 0.3 us)
Async XLA Ops:
  7.2 3.2 %copy-start.2 = (s32[16]{0:T(128)S(1)}, s32[16]{0:T(128)}, u32[]{:S(2)}) copy-start(s32[16]{0:T(128)} %param.14) | copy-start | bytes 196
  7.2 3.6 %copy-start.1 = (bf16[4096]{0:T(1024)(128)(2,1)S(1)}, bf16[4096]{0:T(1024)(128)(2,1)}, u32[]{:S(2)}) copy-start(bf16[4096]{0:T(1024)(128)(2,1)} %param.9) | copy-start | bytes 24580
  7.2 50.8 %all-gather.2.cloned.1.call-start = ((), (), s32[]{:S(2)}) async-start(), calls=%async_computation.2 | async-start | bytes 4456448 | tf_op jit(solution)/shard_map/all_gather | solution.py:157
  10.8 4.0 %copy-start = (bf16[512,4096]{1,0:T(8,128)(2,1)S(1)}, bf16[512,4096]{1,0:T(8,128)(2,1)}, u32[]{:S(2)}) copy-start(bf16[512,4096]{1,0:T(8,128)(2,1)} %param.8) | copy-start | bytes 12582916
  80.6 35.4 %all-to-all-start.1 = ((bf16[8,32,4096]{2,1,0:T(8,128)(2,1)}), bf16[8,32,4096]{2,1,0:T(8,128)(2,1)S(1)}, u32[]{:S(2)}, u32[]{:S(2)}) async-start(bf16[8,32,4096]{2,1,0:T(8,128)(2,1)} %bitcast.39), calls=%async_computation.1 | async-start | bytes 4194304 | tf_op jit(solution)/shard_map/all_to_all | solution.py:184
  111.2 9.3 %copy-start.3 = (s32[64]{0:T(128)S(1)}, s32[64]{0:T(128)}, u32[]{:S(2)}) copy-start(s32[64]{0:T(128)} %param.15) | copy-start | bytes 772
  116.1 32.4 %all-to-all-start = ((bf16[8,32,4096]{2,1,0:T(8,128)(2,1)}), bf16[8,32,4096]{2,1,0:T(8,128)(2,1)}, u32[]{:S(2)}, u32[]{:S(2)}) async-start(bf16[8,32,4096]{2,1,0:T(8,128)(2,1)} %bitcast.38), calls=%async_computation | async-start | bytes 4194304 | tf_op jit(solution)/shard_map/all_to_all | solution.py:184
Sparse Core Ops, SparseCore 0:
  19.5 38.4 all-gather.1
where the time goes:
time: 160 us; the launch traced here: 158 us
  waiting for transfers between devices  42.3 us (26%)
  Pallas kernels  35.3 us (22%)
  between operations  27.2 us (17%)
  matrix products  22.2 us (14%)
  other arithmetic  11.5 us (7%)
  starting transfers between devices  11 us (7%)
  local copies, waits for them, and re-layouts  8.57 us (5%)
    pallas_call x2, Pallas kernels, flash_attention(): pl.pallas_call(flash_kernel, grid_spec=grid_spec, out_shape=jax.ShapeDtyp...  35.3 us
    all_to_all x2, waiting for transfers between devices, on_device(): lax.all_to_all(partial_out, ('tpz', 'tpx'), split_axis=0, concat_axis=0,...  27.8 us
    all_gather x1, waiting for transfers between devices, on_device(): gathered = lax.all_gather(keys_values, 'seq', axis=0, tiled=True)  14.4 us
    all_to_all x2, starting transfers between devices, on_device(): lax.all_to_all(partial_out, ('tpz', 'tpx'), split_axis=0, concat_axis=0,...  10.9 us
    dot_general x2, matrix products, on_device(): jnp.dot(heads_out, w_out, preferred_element_type=jnp.float32)  9.73 us
    dot_general x1, matrix products, on_device(): jnp.dot(normed, w_query, preferred_element_type=jnp.float32)  5.96 us
    dot_general x1, matrix products, on_device(): jnp.dot(normed, value_columns, preferred_element_type=jnp.float32)  3.94 us
  transfers between devices with their start and end apart: 3, of which 3 were waited for; matrix products, arithmetic and copies ran while one was open for 14% of the time, Pallas kernels for 11%

commit v1 on v0

--- a/solution.py
+++ b/solution.py
@@ -181,6 +181,11 @@
         partial_out = jnp.dot(heads_out, w_out, preferred_element_type=jnp.float32).astype(
             jnp.bfloat16
         )
+        if len(outputs) + 1 < CHUNKS:
+            outputs.append(
+                lax.psum_scatter(partial_out, ("tpz", "tpx"), scatter_dimension=0, tiled=True)
+            )
+            continue
         received = lax.all_to_all(
             partial_out, ("tpz", "tpx"), split_axis=0, concat_axis=0, tiled=True
         ).reshape(tp_count, piece, -1)

time: 160 us -> 185 us (1.16); the launches traced: 158 us -> 187 us
  waiting for transfers between devices: 42.3 us -> 75.7 us
  starting transfers between devices: 11 us -> 6.78 us
    reduce_scatter x0 -> x1, waiting for transfers between devices: none -> 31.9 us  [on_device(): lax.psum_scatter(partial_out, ('tpz', 'tpx'), scatter_dimension=0, tiled=...]
    all_to_all x2 -> x1, starting transfers between devices: 10.9 us -> 6.7 us  [on_device(): lax.all_to_all(partial_out, ('tpz', 'tpx'), split_axis=0, concat_axis=0,...]
    all_to_all x2 -> x1, waiting for transfers between devices: 27.8 us -> 29.6 us  [on_device(): lax.all_to_all(partial_out, ('tpz', 'tpx'), split_axis=0, concat_axis=0,...]
  transfers between devices with their start and end apart: 3 -> 3, of which waited for: 3 -> 3; matrix products, arithmetic and copies ran while one was open for 14% -> 12% of each run, Pallas kernels for 11% -> 9%
where the time goes in v1:
time: 185 us; the launch traced here: 187 us
  waiting for transfers between devices  75.7 us (41%)
  Pallas kernels  35.5 us (19%)
  between operations  27.2 us (15%)
  matrix products  22.2 us (12%)
  other arithmetic  10.7 us (6%)
  local copies, waits for them, and re-layouts  8.65 us (5%)
  starting transfers between devices  6.78 us (4%)
    pallas_call x2, Pallas kernels, flash_attention(): pl.pallas_call(flash_kernel, grid_spec=grid_spec, out_shape=jax.ShapeDtyp...  35.5 us
    reduce_scatter x1, waiting for transfers between devices, on_device(): lax.psum_scatter(partial_out, ('tpz', 'tpx'), scatter_dimension=0, tiled=...  31.9 us
    all_to_all x1, waiting for transfers between devices, on_device(): lax.all_to_all(partial_out, ('tpz', 'tpx'), split_axis=0, concat_axis=0,...  29.6 us
    all_gather x1, waiting for transfers between devices, on_device(): gathered = lax.all_gather(keys_values, 'seq', axis=0, tiled=True)  14.2 us
    dot_general x2, matrix products, on_device(): jnp.dot(heads_out, w_out, preferred_element_type=jnp.float32)  9.78 us
    all_to_all x1, starting transfers between devices, on_device(): lax.all_to_all(partial_out, ('tpz', 'tpx'), split_axis=0, concat_axis=0,...  6.7 us
    dot_general x1, matrix products, on_device(): jnp.dot(normed, w_query, preferred_element_type=jnp.float32)  5.97 us
    dot_general x1, matrix products, on_device(): jnp.dot(normed, value_columns, preferred_element_type=jnp.float32)  3.94 us
  transfers between devices with their start and end apart: 3, of which 3 were waited for; matrix products, arithmetic and copies ran while one was open for 12% of the time, Pallas kernels for 9%

profile of v1, /device:TPU:24, one launch (start us, length us, event | category | flops | bytes accessed | tf_op | source)
XLA Modules:
  0.0 186.7 jit_solution(10140134388781892995)
XLA Ops:
  7.3 3.1 %fusion = f32[512]{0:T(512)S(1)} fusion(bf16[512,4096]{1,0:T(8,128)(2,1)} %param.8), kind=kLoop, calls=%fused_computation.2 | loop fusion | flops 6290944 | bytes 4196352 | tf_op jit(solution)/shard_map/reduce_sum | solution.py:43
  10.4 0.1 copy.32
  10.5 0.1 reduce
  10.6 0.1 select_reduce_fusion
  10.8 3.9 %convolution_convert_fusion.2 = bf16[512,128]{1,0:T(8,128)(2,1)S(1)} fusion(bf16[4096,512]{1,0:T(8,128)(2,1)} %param.12, s32[]{:T(128)S(6)} %select_n.61, bf16[512,4096]{1,0:T(8,128)(2,1)} %param.8, f32[4096]{0:T(1024)S(1)} %convert_element_type.72, f32[512]{0:T(512)S(1)} %add_rsqrt_fusion), kind=kOutput, calls=%fused_computation.8 | convolution fusion | flops 545325056 | bytes 5392388 | tf_op jit(solution)/shard_map/dot_general | solution.py:153
  14.7 2.5 %convolution_bitcast_fusion = f32[512,1,128]{2,0,1:T(8,128)S(1)} fusion(bf16[4096,512]{1,0:T(8,128)(2,1)} %param.11, s32[]{:T(128)S(6)} %select_n.61, bf16[512,4096]{1,0:T(8,128)(2,1)S(1)} %copy-done, f32[4096]{0:T(1024)S(1)} %convert_element_type.72, f32[512]{0:T(512)S(1)} %add_rsqrt_fusion), kind=kOutput, calls=%fused_computation.7 | convolution fusion | flops 545259520 | bytes 5523460 | tf_op jit(solution)/shard_map/dot_general | solution.py:151
  17.3 1.2 fusion.10
  18.5 0.1 maximum_bitcast_fusion
  18.6 0.7 pad_maximum_fusion.2
  19.4 0.0 reduce-scatter.2.cloned.1.call-start
  19.4 0.1 reshape.237
  19.5 0.1 reshape_squeeze.23
  19.6 0.1 broadcast_in_dim_reshape_squeeze.15
  19.7 0.1 reshape_squeeze.20
  19.8 0.1 broadcast_in_dim_reshape_squeeze.13
  19.9 0.1 reshape_squeeze.22
  19.9 0.6 fusion.22
  25.7 0.1 reshape_squeeze.19
  25.8 0.7 fusion.24
  31.7 0.1 broadcast_in_dim_reshape_squeeze.14
  31.7 0.1 broadcast_in_dim_reshape_squeeze.12
  31.8 6.0 %fusion.17 = f32[512,512]{0,1:T(8,128)S(1)} fusion(bf16[4096,512]{1,0:T(8,128)(2,1)} %param.10, bf16[512,4096]{1,0:T(8,128)(2,1)} %param.8, f32[4096]{0:T(1024)S(1)} %convert_element_type.72, f32[512]{0:T(512)S(1)} %add_rsqrt_fusion), kind=kOutput, calls=%fused_computation.47 | convolution fusion | flops 2155872256 | bytes 9455616 | tf_op jit(solution)/shard_map/dot_general | solution.py:160
  37.8 0.1 fusion.19
  37.9 0.4 copy.44
  38.3 0.4 copy.43
  38.7 1.0 multiply_cosine_fusion.1
  39.7 0.6 subtract_convert_fusion
  40.3 0.7 pad_maximum_fusion
  41.0 0.2 convert_element_type.75
  41.3 0.8 fusion.20
  42.1 0.8 copy.37.start_ref
  42.9 0.8 copy.38.index_ref
  43.7 14.2 %all-gather.2.cloned.1.call-done.kv_ref = bf16[8192,256]{1,0:T(8,128)(2,1)} async-done(((bf16[512,256]{1,0:T(8,128)(2,1)}), bf16[8192,256]{1,0:T(8,128)(2,1)}) %all-gather.2.cloned.1.call-update) | async-done | bytes 4194320 | tf_op jit(solution)/shard_map/all_gather | solution.py:157
  57.9 17.9 %shard_map.95 = bf16[256,512]{1,0:T(8,128)(2,1)} custom-call(s32[1]{0:T(128)S(6)} %select_n.56.lo_ref, s32[1]{0:T(128)S(6)} %select_n.57.hi_ref, s32[1]{0:T(128)} %get-tuple-element.18.base_ref, s32[1]{0:T(128)} %get-tuple-element.19.last_start_ref, bf16[256,512]{1,0:T(8,128)(2,1)} %bitcast.41, s32[256,1]{1,0:T(8,128)} %copy.37.start_ref, ...), custom_call_target="tpu_custom_call" | custom-call | tf_op jit(solution)/shard_map/pallas_call | solution.py:127
  75.8 4.9 %convolution_convert_fusion.1 = bf16[256,4096]{1,0:T(8,128)(2,1)} fusion(bf16[256,512]{1,0:T(8,128)(2,1)} %shard_map.95, bf16[512,4096]{1,0:T(8,128)(2,1)} %param.13), kind=kOutput, calls=%fused_computation.6 | convolution fusion | flops 1074790400 | bytes 6553600 | tf_op jit(solution)/shard_map/dot_general | solution.py:181
  80.7 0.8 copy.39.start_ref
  81.5 0.8 copy.40.index_ref
  82.3 17.6 %shard_map.96 = bf16[256,512]{1,0:T(8,128)(2,1)} custom-call(s32[1]{0:T(128)S(6)} %select_n.58.lo_ref, s32[1]{0:T(128)S(6)} %select_n.59.hi_ref, s32[1]{0:T(128)} %get-tuple-element.25.base_ref, s32[1]{0:T(128)} %get-tuple-element.26.last_start_ref, bf16[256,512]{1,0:T(8,128)(2,1)} %bitcast.40, s32[256,1]{1,0:T(8,128)} %copy.39.start_ref, ...), custom_call_target="tpu_custom_call" | custom-call | tf_op jit(solution)/shard_map/pallas_call | solution.py:127
  99.9 4.9 %convolution_convert_fusion = bf16[256,4096]{1,0:T(8,128)(2,1)} fusion(bf16[256,512]{1,0:T(8,128)(2,1)} %shard_map.96, bf16[512,4096]{1,0:T(8,128)(2,1)} %param.13), kind=kOutput, calls=%fused_computation.5 | convolution fusion | flops 1074790400 | bytes 6553600 | tf_op jit(solution)/shard_map/dot_general | solution.py:181
  104.8 6.7 %all-to-all-start = ((bf16[8,32,4096]{2,1,0:T(8,128)(2,1)}), bf16[8,32,4096]{2,1,0:T(8,128)(2,1)S(1)}, u32[]{:S(2)}, u32[]{:S(2)}) async-start(bf16[8,32,4096]{2,1,0:T(8,128)(2,1)} %bitcast.38), calls=%async_computation.1 | async-start | bytes 4194304 | tf_op jit(solution)/shard_map/all_to_all | solution.py:189
  111.5 0.2 select_reduce_fusion.1
  111.7 0.6 fusion.26
  114.9 0.8 dynamic-slice_bitcast_fusion.3
  115.7 0.7 pad_maximum_fusion.3
  116.4 29.6 %all-to-all-done = bf16[8,32,4096]{2,1,0:T(8,128)(2,1)S(1)} async-done(((bf16[8,32,4096]{2,1,0:T(8,128)(2,1)}), bf16[8,32,4096]{2,1,0:T(8,128)(2,1)S(1)}, u32[]{:S(2)}, u32[]{:S(2)}) %all-to-all-start) | async-done | bytes 2097184 | tf_op jit(solution)/shard_map/all_to_all | solution.py:189
  146.0 0.3 add_convert_fusion.1
  146.2 31.9 %reduce-scatter.2.cloned.1.call-done = bf16[32,4096]{1,0:T(8,128)(2,1)} async-done(((bf16[256,4096]{1,0:T(8,128)(2,1)}), bf16[32,4096]{1,0:T(8,128)(2,1)}) %reduce-scatter.2.cloned.1.call-update) | async-done | bytes 262160 | tf_op jit(solution)/shard_map/reduce_scatter | solution.py:186
  178.1 1.8 pad_maximum_fusion.1
  (21 shorter events, 0.2 us)
Async XLA Ops:
  7.2 3.2 %copy-start.2 = (s32[16]{0:T(128)S(1)}, s32[16]{0:T(128)}, u32[]{:S(2)}) copy-start(s32[16]{0:T(128)} %param.14) | copy-start | bytes 196
  7.2 3.6 %copy-start.1 = (bf16[4096]{0:T(1024)(128)(2,1)S(1)}, bf16[4096]{0:T(1024)(128)(2,1)}, u32[]{:S(2)}) copy-start(bf16[4096]{0:T(1024)(128)(2,1)} %param.9) | copy-start | bytes 24580
  7.2 50.8 %all-gather.2.cloned.1.call-start = ((), (), s32[]{:S(2)}) async-start(), calls=%async_computation.2 | async-start | bytes 4456448 | tf_op jit(solution)/shard_map/all_gather | solution.py:157
  10.8 4.0 %copy-start = (bf16[512,4096]{1,0:T(8,128)(2,1)S(1)}, bf16[512,4096]{1,0:T(8,128)(2,1)}, u32[]{:S(2)}) copy-start(bf16[512,4096]{1,0:T(8,128)(2,1)} %param.8) | copy-start | bytes 12582916
  19.4 158.7 %reduce-scatter.2.cloned.1.call-start = ((), (), s32[]{:S(2)}) async-start(), calls=%async_computation.3 | async-start | bytes 2359296 | tf_op jit(solution)/shard_map/reduce_scatter | solution.py:186
  104.8 6.7 %copy-start.3 = (s32[64]{0:T(128)S(1)}, s32[64]{0:T(128)}, u32[]{:S(2)}) copy-start(s32[64]{0:T(128)} %param.15) | copy-start | bytes 772
  104.8 41.2 %all-to-all-start = ((bf16[8,32,4096]{2,1,0:T(8,128)(2,1)}), bf16[8,32,4096]{2,1,0:T(8,128)(2,1)S(1)}, u32[]{:S(2)}, u32[]{:S(2)}) async-start(bf16[8,32,4096]{2,1,0:T(8,128)(2,1)} %bitcast.38), calls=%async_computation.1 | async-start | bytes 4194304 | tf_op jit(solution)/shard_map/all_to_all | solution.py:189
Sparse Core Ops, SparseCore 0:
  19.5 38.4 all-gather.1
  80.8 97.2 reduce-scatter.1

commit v2 on v0

--- a/solution.py
+++ b/solution.py
@@ -167,17 +167,24 @@
     chunk_queries = queries.reshape(tp_count, CHUNKS, piece, heads_here * HD)
     chunk_start = start.reshape(tp_count, CHUNKS, piece)
     chunk_index = token_index.reshape(tp_count, CHUNKS, piece)
-    chunk_inputs = []
-    for c in range(CHUNKS):
-        q_rows = chunk_queries[:, c].reshape(tp_count * piece, heads_here * HD)
-        s_rows = chunk_start[:, c].reshape(tp_count * piece)
-        i_rows = chunk_index[:, c].reshape(tp_count * piece)
+    seq_count = lax.axis_size("seq")
+    swap = [(r, seq_count - 1 - r) for r in range(seq_count)]
+    partner_index = (seq_count - 1 - seq_rank) * row_count + jnp.arange(row_count, dtype=jnp.int32)
+    partner_start = segment_start(partner_index, prompt_lengths)
+    partner_start = partner_start.reshape(tp_count, CHUNKS, piece)
+    partner_index = partner_index.reshape(tp_count, CHUNKS, piece)
+
+    def kernel_inputs(q_rows, s_rows, i_rows):
+        s_rows = s_rows.reshape(tp_count * piece)
+        i_rows = i_rows.reshape(tp_count * piece)
         bounds = (s_rows[:1] // BK, i_rows[-1:] // BK, i_rows[:1], s_rows[-1:])
-        chunk_inputs.append((q_rows, s_rows[:, None], i_rows[:, None], bounds))
-    chunk_inputs = lax.optimization_barrier(chunk_inputs)
-    outputs = []
-    for q_rows, s_rows, i_rows, bounds in chunk_inputs:
-        heads_out = flash_attention(q_rows, s_rows, i_rows, gathered, bounds)
+        return (q_rows.reshape(tp_count * piece, heads_here * HD), s_rows[:, None], i_rows[:, None], bounds)
+
+    sent_queries = lax.ppermute(chunk_queries[:, 1], "seq", swap)
+    own_inputs = kernel_inputs(chunk_queries[:, 0], chunk_start[:, 0], chunk_index[:, 0])
+    partner_inputs = kernel_inputs(sent_queries, partner_start[:, 1], partner_index[:, 1])
+    own_inputs, partner_inputs = lax.optimization_barrier((own_inputs, partner_inputs))
+    def reduce_over_tp(heads_out):
         partial_out = jnp.dot(heads_out, w_out, preferred_element_type=jnp.float32).astype(
             jnp.bfloat16
         )
@@ -187,7 +194,13 @@
         summed = received[0].astype(jnp.float32)
         for t in range(1, tp_count):
             summed = summed + received[t].astype(jnp.float32)
-        outputs.append(summed.astype(jnp.bfloat16))
+        return summed.astype(jnp.bfloat16)
+
+    partner_heads = flash_attention(*partner_inputs[:3], gathered, partner_inputs[3])
+    partner_heads, own_inputs = lax.optimization_barrier((partner_heads, own_inputs))
+    returned = lax.ppermute(reduce_over_tp(partner_heads), "seq", swap)
+    own_heads = flash_attention(*own_inputs[:3], gathered, own_inputs[3])
+    outputs = [reduce_over_tp(own_heads), returned]
     attended = jnp.stack(outputs, axis=0).reshape(-1, outputs[0].shape[1])
 
     cache_width = 2 * HD // sharing

time: 160 us -> 168 us (1.050)
  the two profiles are of different devices: /device:TPU:24 before, /device:TPU:2 now
where the time goes in v2:
time: 168 us; the launch traced here: 166 us
  waiting for transfers between devices  54.7 us (33%)
  Pallas kernels  27.5 us (16%)
  between operations  27.3 us (16%)
  matrix products  22.2 us (13%)
  starting transfers between devices  13.1 us (8%)
  other arithmetic  11.5 us (7%)
  local copies, waits for them, and re-layouts  9.24 us (6%)
    all_to_all x2, waiting for transfers between devices, reduce_over_tp(): lax.all_to_all(partial_out, ('tpz', 'tpx'), split_axis=0, concat_axis=0,...  37.4 us
    pallas_call x2, Pallas kernels, flash_attention(): pl.pallas_call(flash_kernel, grid_spec=grid_spec, out_shape=jax.ShapeDtyp...  27.5 us
    all_gather x1, waiting for transfers between devices, on_device(): gathered = lax.all_gather(keys_values, 'seq', axis=0, tiled=True)  16.8 us
    all_to_all x2, starting transfers between devices, reduce_over_tp(): lax.all_to_all(partial_out, ('tpz', 'tpx'), split_axis=0, concat_axis=0,...  10.5 us
    dot_general x2, matrix products, reduce_over_tp(): jnp.dot(heads_out, w_out, preferred_element_type=jnp.float32)  9.73 us
    dot_general x1, matrix products, on_device(): jnp.dot(normed, w_query, preferred_element_type=jnp.float32)  5.93 us
    dot_general x1, matrix products, on_device(): jnp.dot(normed, value_columns, preferred_element_type=jnp.float32)  3.94 us
  transfers between devices with their start and end apart: 5, of which 4 were waited for; matrix products, arithmetic and copies ran while one was open for 15% of the time, Pallas kernels for 6%

profile of v2, /device:TPU:2, one launch (start us, length us, event | category | flops | bytes accessed | tf_op | source)
XLA Modules:
  0.0 165.5 jit_solution(1688414498157235950)
XLA Ops:
  7.3 3.1 %fusion = f32[512]{0:T(512)S(1)} fusion(bf16[512,4096]{1,0:T(8,128)(2,1)} %param.8), kind=kLoop, calls=%fused_computation.2 | loop fusion | flops 6290944 | bytes 4196352 | tf_op jit(solution)/shard_map/reduce_sum | solution.py:43
  10.4 0.1 copy.32
  10.5 0.1 reduce
  10.6 0.1 select_reduce_fusion
  10.8 3.9 %convolution_convert_fusion.2 = bf16[512,128]{1,0:T(8,128)(2,1)S(1)} fusion(bf16[4096,512]{1,0:T(8,128)(2,1)} %param.12, s32[]{:T(128)S(6)} %select_n.65, bf16[512,4096]{1,0:T(8,128)(2,1)} %param.8, f32[4096]{0:T(1024)S(1)} %convert_element_type.115, f32[512]{0:T(512)S(1)} %add_rsqrt_fusion), kind=kOutput, calls=%fused_computation.8 | convolution fusion | flops 545325056 | bytes 5392388 | tf_op jit(solution)/shard_map/dot_general | solution.py:153
  14.7 2.5 %convolution_bitcast_fusion = f32[512,1,128]{2,0,1:T(8,128)S(1)} fusion(bf16[4096,512]{1,0:T(8,128)(2,1)} %param.11, s32[]{:T(128)S(6)} %select_n.65, bf16[512,4096]{1,0:T(8,128)(2,1)S(1)} %copy-done, f32[4096]{0:T(1024)S(1)} %convert_element_type.115, f32[512]{0:T(512)S(1)} %add_rsqrt_fusion), kind=kOutput, calls=%fused_computation.7 | convolution fusion | flops 545259520 | bytes 5523460 | tf_op jit(solution)/shard_map/dot_general | solution.py:151
  17.3 1.2 fusion.10
  18.5 0.1 maximum_bitcast_fusion
  18.7 0.7 pad_maximum_fusion.2
  19.4 5.9 %fusion.18 = f32[512,512]{0,1:T(8,128)S(1)} fusion(bf16[4096,512]{1,0:T(8,128)(2,1)} %param.10, bf16[512,4096]{1,0:T(8,128)(2,1)} %param.8, f32[4096]{0:T(1024)S(1)} %convert_element_type.115, f32[512]{0:T(512)S(1)} %add_rsqrt_fusion), kind=kOutput, calls=%fused_computation.54 | convolution fusion | flops 2155872256 | bytes 9455616 | tf_op jit(solution)/shard_map/dot_general | solution.py:160
  25.3 0.1 fusion.20
  25.5 0.4 copy.44
  25.9 0.4 copy.43
  26.3 1.0 multiply_cosine_fusion.1
  27.2 0.6 subtract_convert_fusion
  27.9 0.7 pad_maximum_fusion
  28.6 0.2 convert_element_type.118
  28.8 0.8 slice_bitcast_fusion
  29.5 2.4 %collective-permute-start = (bf16[8,32,512]{2,1,0:T(8,128)(2,1)S(1)}, bf16[8,32,512]{2,1,0:T(8,128)(2,1)S(1)}, u32[]{:S(2)}, u32[]{:S(2)}) collective-permute-start(bf16[8,32,512]{2,1,0:T(8,128)(2,1)S(1)} %get-tuple-element.56), channel_id=1, source_target_pairs={{0,120},{8,112},{16,104},{24,96},{32,88},{40,80},{48,72},{56,64},{... | collective-permute-start | bytes 786440 | tf_op jit(solution)/shard_map/ppermute | solution.py:183
  32.0 0.1 reshape.291
  32.0 0.1 reshape.293
  32.2 0.6 fusion.23
  34.8 0.1 reshape_squeeze.16
  34.9 0.6 fusion.25
  39.2 0.6 fusion.24
  45.0 0.1 broadcast_in_dim_reshape_squeeze.14
  45.2 0.5 collective-permute-done
  45.7 0.8 copy.37.start_ref
  46.5 0.8 copy.38.index_ref
  47.3 16.8 %all-gather.2.cloned.1.call-done.kv_ref = bf16[8192,256]{1,0:T(8,128)(2,1)} async-done(((bf16[512,256]{1,0:T(8,128)(2,1)}), bf16[8192,256]{1,0:T(8,128)(2,1)}) %all-gather.2.cloned.1.call-update) | async-done | bytes 4194320 | tf_op jit(solution)/shard_map/all_gather | solution.py:157
  64.0 17.8 %shard_map.95 = bf16[256,512]{1,0:T(8,128)(2,1)} custom-call(s32[1]{0:T(128)S(6)} %select_n.62.lo_ref, s32[1]{0:T(128)S(6)} %select_n.63.hi_ref, s32[1]{0:T(128)} %get-tuple-element.26.base_ref, s32[1]{0:T(128)} %get-tuple-element.27.last_start_ref, bf16[256,512]{1,0:T(8,128)(2,1)} %bitcast.48, s32[256,1]{1,0:T(8,128)} %copy.37.start_ref, ...), custom_call_target="tpu_custom_call" | custom-call | tf_op jit(solution)/shard_map/pallas_call | solution.py:127
  81.8 4.9 %convolution_convert_fusion = bf16[256,4096]{1,0:T(8,128)(2,1)} fusion(bf16[256,512]{1,0:T(8,128)(2,1)} %shard_map.95, bf16[512,4096]{1,0:T(8,128)(2,1)} %param.13), kind=kOutput, calls=%fused_computation.5 | convolution fusion | flops 1074790400 | bytes 6553600 | tf_op jit(solution)/shard_map/dot_general | solution.py:188
  86.7 6.2 %all-to-all-start.1 = ((bf16[8,32,4096]{2,1,0:T(8,128)(2,1)}), bf16[8,32,4096]{2,1,0:T(8,128)(2,1)S(1)}, u32[]{:S(2)}, u32[]{:S(2)}) async-start(bf16[8,32,4096]{2,1,0:T(8,128)(2,1)} %bitcast.44), calls=%async_computation.1 | async-start | bytes 4194304 | tf_op jit(solution)/shard_map/all_to_all | solution.py:191
  92.9 0.8 copy.39.start_ref
  93.7 0.8 copy.40.index_ref
  94.5 9.8 %shard_map.96 = bf16[256,512]{1,0:T(8,128)(2,1)} custom-call(s32[1]{0:T(128)S(6)} %select_n.59.lo_ref, s32[1]{0:T(128)S(6)} %select_n.60.hi_ref, s32[1]{0:T(128)} %get-tuple-element.40.base_ref, s32[1]{0:T(128)} %get-tuple-element.41.last_start_ref, bf16[256,512]{1,0:T(8,128)(2,1)} %bitcast.46, s32[256,1]{1,0:T(8,128)} %copy.39.start_ref, ...), custom_call_target="tpu_custom_call" | custom-call | tf_op jit(solution)/shard_map/pallas_call | solution.py:127
  104.2 4.8 %convolution_convert_fusion.1 = bf16[256,4096]{1,0:T(8,128)(2,1)} fusion(bf16[256,512]{1,0:T(8,128)(2,1)} %shard_map.96, bf16[512,4096]{1,0:T(8,128)(2,1)} %param.13), kind=kOutput, calls=%fused_computation.6 | convolution fusion | flops 1074790400 | bytes 6553600 | tf_op jit(solution)/shard_map/dot_general | solution.py:188
  109.1 12.7 %all-to-all-done.1 = bf16[8,32,4096]{2,1,0:T(8,128)(2,1)S(1)} async-done(((bf16[8,32,4096]{2,1,0:T(8,128)(2,1)}), bf16[8,32,4096]{2,1,0:T(8,128)(2,1)S(1)}, u32[]{:S(2)}, u32[]{:S(2)}) %all-to-all-start.1) | async-done | bytes 2097184 | tf_op jit(solution)/shard_map/all_to_all | solution.py:191
  121.8 4.4 %all-to-all-start = ((bf16[8,32,4096]{2,1,0:T(8,128)(2,1)}), bf16[8,32,4096]{2,1,0:T(8,128)(2,1)}, u32[]{:S(2)}, u32[]{:S(2)}) async-start(bf16[8,32,4096]{2,1,0:T(8,128)(2,1)} %bitcast.43), calls=%async_computation | async-start | bytes 4194304 | tf_op jit(solution)/shard_map/all_to_all | solution.py:191
  126.1 0.2 select_reduce_fusion.2
  126.3 0.6 fusion.27
  129.5 0.8 dynamic-slice_bitcast_fusion.3
  130.3 0.7 pad_maximum_fusion.3
  131.0 0.3 fusion.13
  131.3 0.1 collective-permute-start.1
  131.3 24.7 %all-to-all-done = bf16[8,32,4096]{2,1,0:T(8,128)(2,1)} async-done(((bf16[8,32,4096]{2,1,0:T(8,128)(2,1)}), bf16[8,32,4096]{2,1,0:T(8,128)(2,1)}, u32[]{:S(2)}, u32[]{:S(2)}) %all-to-all-start) | async-done | bytes 2097184 | tf_op jit(solution)/shard_map/all_to_all | solution.py:191
  156.0 1.8 %add_convert_fusion.2 = bf16[1,32,4096]{2,1,0:T(8,128)(2,1)S(1)} fusion(bf16[8,32,4096]{2,1,0:T(8,128)(2,1)} %all-to-all-done), kind=kLoop, calls=%fused_computation.16 | loop fusion | flops 2097152 | bytes 2359296 | tf_op jit(solution)/shard_map/convert_element_type | solution.py:197
  157.8 0.8 pad_maximum_fusion.1
  (30 shorter events, 0.7 us)
Async XLA Ops:
  7.2 3.2 %copy-start.3 = (s32[16]{0:T(128)S(1)}, s32[16]{0:T(128)}, u32[]{:S(2)}) copy-start(s32[16]{0:T(128)} %param.14) | copy-start | bytes 196
  7.2 3.6 %copy-start.2 = (bf16[4096]{0:T(1024)(128)(2,1)S(1)}, bf16[4096]{0:T(1024)(128)(2,1)}, u32[]{:S(2)}) copy-start(bf16[4096]{0:T(1024)(128)(2,1)} %param.9) | copy-start | bytes 24580
  7.2 56.9 %all-gather.2.cloned.1.call-start = ((), (), s32[]{:S(2)}) async-start(), calls=%async_computation.2 | async-start | bytes 4456448 | tf_op jit(solution)/shard_map/all_gather | solution.py:157
  10.8 4.0 %copy-start = (bf16[512,4096]{1,0:T(8,128)(2,1)S(1)}, bf16[512,4096]{1,0:T(8,128)(2,1)}, u32[]{:S(2)}) copy-start(bf16[512,4096]{1,0:T(8,128)(2,1)} %param.8) | copy-start | bytes 12582916
  29.5 16.1 %collective-permute-start = (bf16[8,32,512]{2,1,0:T(8,128)(2,1)S(1)}, bf16[8,32,512]{2,1,0:T(8,128)(2,1)S(1)}, u32[]{:S(2)}, u32[]{:S(2)}) collective-permute-start(bf16[8,32,512]{2,1,0:T(8,128)(2,1)S(1)} %get-tuple-element.56), channel_id=1, source_target_pairs={{0,120},{8,112},{16,104},{24,96},{32,88},{40,80},{48,72},{56,64},{... | collective-permute-start | bytes 786440 | tf_op jit(solution)/shard_map/ppermute | solution.py:183
  45.7 18.4 %copy-start.1 = (bf16[8,32,512]{2,1,0:T(8,128)(2,1)}, bf16[8,32,512]{2,1,0:T(8,128)(2,1)S(1)}, u32[]{:S(2)}) copy-start(bf16[8,32,512]{2,1,0:T(8,128)(2,1)S(1)} %collective-permute-done) | copy-start | bytes 786436
  86.7 35.1 %all-to-all-start.1 = ((bf16[8,32,4096]{2,1,0:T(8,128)(2,1)}), bf16[8,32,4096]{2,1,0:T(8,128)(2,1)S(1)}, u32[]{:S(2)}, u32[]{:S(2)}) async-start(bf16[8,32,4096]{2,1,0:T(8,128)(2,1)} %bitcast.44), calls=%async_computation.1 | async-start | bytes 4194304 | tf_op jit(solution)/shard_map/all_to_all | solution.py:191
  109.1 17.0 %copy-start.4 = (s32[64]{0:T(128)S(1)}, s32[64]{0:T(128)}, u32[]{:S(2)}) copy-start(s32[64]{0:T(128)} %param.15) | copy-start | bytes 772
  121.8 34.3 %all-to-all-start = ((bf16[8,32,4096]{2,1,0:T(8,128)(2,1)}), bf16[8,32,4096]{2,1,0:T(8,128)(2,1)}, u32[]{:S(2)}, u32[]{:S(2)}) async-start(bf16[8,32,4096]{2,1,0:T(8,128)(2,1)} %bitcast.43), calls=%async_computation | async-start | bytes 4194304 | tf_op jit(solution)/shard_map/all_to_all | solution.py:191
  131.3 26.6 %collective-permute-start.1 = (bf16[32,4096]{1,0:T(8,128)(2,1)S(1)}, bf16[32,4096]{1,0:T(8,128)(2,1)S(1)}, u32[]{:S(2)}, u32[]{:S(2)}) collective-permute-start(bf16[32,4096]{1,0:T(8,128)(2,1)S(1)} %fusion.13), channel_id=1, source_target_pairs={{0,120},{8,112},{16,104},{24,96},{32,88},{40,80},{48,72},{56,64},{... | collective-permute-start | bytes 786440 | tf_op jit(solution)/shard_map/ppermute | solution.py:201
Sparse Core Ops, SparseCore 0:
  19.5 44.4 all-gather.1

commit v3 on v0

--- a/solution.py
+++ b/solution.py
@@ -44,7 +44,7 @@
     return (hidden * factor * norm_gain.astype(jnp.float32)).astype(jnp.bfloat16)
 
 
-def flash_kernel(lo_ref, hi_ref, base_ref, last_start_ref, q_ref, start_ref, index_ref, kv_ref, o_ref):
+def flash_kernel(lo_ref, hi_ref, base_ref, last_start_ref, q_ref, start_ref, index_ref, kv_ref, w_ref, o_ref):
     i = pl.program_id(0)
     heads = q_ref.shape[1] // HD
     row_index = index_ref[...]
@@ -103,15 +103,22 @@
 
     carry = lax.fori_loop(0, before + hi - mid_hi, masked_step, carry)
     carry = lax.fori_loop(mid_lo, mid_hi, functools.partial(step, masked=False), carry)
-    for h in range(heads):
-        running_max, running_sum, weighted = carry[h]
-        o_ref[:, pl.ds(h * HD, HD)] = (weighted / running_sum).astype(o_ref.dtype)
-
-
-def flash_attention(queries, row_start, row_index, key_values, bounds):
+    heads_out = jnp.concatenate(
+        [(weighted / running_sum).astype(jnp.bfloat16) for _, running_sum, weighted in carry],
+        axis=1,
+    )
+    tile = 512
+    for n in range(o_ref.shape[1] // tile):
+        o_ref[:, pl.ds(n * tile, tile)] = jnp.dot(
+            heads_out, w_ref[:, pl.ds(n * tile, tile)], preferred_element_type=jnp.float32
+        ).astype(o_ref.dtype)
+
+
+def flash_attention(queries, row_start, row_index, key_values, w_out, bounds):
     rows, width = queries.shape
     q_blocks = rows // BQ
     kv_rows = key_values.shape[0]
+    model_width = w_out.shape[1]
     rows_of = lambda i, *_: (i, 0)
     grid_spec = pltpu.PrefetchScalarGridSpec(
         num_scalar_prefetch=4,
@@ -121,14 +128,15 @@
             pl.BlockSpec((BQ, 1), rows_of),
             pl.BlockSpec((BQ, 1), rows_of),
             pl.BlockSpec((kv_rows, 2 * HD), lambda i, *_: (0, 0)),
+            pl.BlockSpec((width, model_width), lambda i, *_: (0, 0)),
         ],
-        out_specs=pl.BlockSpec((BQ, width), rows_of),
+        out_specs=pl.BlockSpec((BQ, model_width), rows_of),
     )
     return pl.pallas_call(
         flash_kernel,
         grid_spec=grid_spec,
-        out_shape=jax.ShapeDtypeStruct((rows, width), jnp.bfloat16),
-    )(*bounds, queries, row_start, row_index, key_values)
+        out_shape=jax.ShapeDtypeStruct((rows, model_width), jnp.bfloat16),
+    )(*bounds, queries, row_start, row_index, key_values, w_out)
 
 
 def on_device(tokens, norm_gain, w_query, w_key, w_value, w_out, prompt_lengths, page_slots):
@@ -177,10 +185,7 @@
     chunk_inputs = lax.optimization_barrier(chunk_inputs)
     outputs = []
     for q_rows, s_rows, i_rows, bounds in chunk_inputs:
-        heads_out = flash_attention(q_rows, s_rows, i_rows, gathered, bounds)
-        partial_out = jnp.dot(heads_out, w_out, preferred_element_type=jnp.float32).astype(
-            jnp.bfloat16
-        )
+        partial_out = flash_attention(q_rows, s_rows, i_rows, gathered, w_out, bounds)
         received = lax.all_to_all(
             partial_out, ("tpz", "tpx"), split_axis=0, concat_axis=0, tiled=True
         ).reshape(tp_count, piece, -1)

time: 160 us -> 160 us (level)
  the two profiles are of different devices: /device:TPU:24 before, /device:TPU:18 now
where the time goes in v3:
time: 160 us; the launch traced here: 157 us
  waiting for transfers between devices  43.8 us (27%)
  Pallas kernels  41.5 us (26%)
  between operations  27.1 us (17%)
  other arithmetic  12.8 us (8%)
  matrix products  12.5 us (8%)
  starting transfers between devices  10.3 us (6%)
  local copies, waits for them, and re-layouts  9.27 us (6%)
    pallas_call x2, Pallas kernels, flash_attention(): pl.pallas_call(flash_kernel, grid_spec=grid_spec, out_shape=jax.ShapeDtyp...  41.5 us
    all_to_all x2, waiting for transfers between devices, on_device(): lax.all_to_all(partial_out, ('tpz', 'tpx'), split_axis=0, concat_axis=0,...  29.5 us
    all_gather x1, waiting for transfers between devices, on_device(): gathered = lax.all_gather(keys_values, 'seq', axis=0, tiled=True)  14.2 us
    all_to_all x2, starting transfers between devices, on_device(): lax.all_to_all(partial_out, ('tpz', 'tpx'), split_axis=0, concat_axis=0,...  10.3 us
    dot_general x1, matrix products, on_device(): jnp.dot(normed, w_query, preferred_element_type=jnp.float32)  6 us
    dot_general x1, matrix products, on_device(): jnp.dot(normed, key_columns, preferred_element_type=jnp.float32)[:, None, :]  3.95 us
  transfers between devices with their start and end apart: 3, of which 3 were waited for; matrix products, arithmetic and copies ran while one was open for 11% of the time, Pallas kernels for 13%

profile of v3, /device:TPU:18, one launch (start us, length us, event | category | flops | bytes accessed | tf_op | source)
XLA Modules:
  0.0 157.2 jit_solution(4532529727083417165)
XLA Ops:
  7.3 0.7 copy.32
  8.0 0.1 reduce
  8.2 0.7 select_reduce_fusion
  8.9 0.7 convert_element_type.102
  9.6 3.1 %fusion = f32[512]{0:T(512)S(1)} fusion(bf16[512,4096]{1,0:T(8,128)(2,1)} %param.8), kind=kLoop, calls=%fused_computation.2 | loop fusion | flops 6290944 | bytes 4196352 | tf_op jit(solution)/shard_map/reduce_sum | solution.py:43
  12.7 3.9 %convolution_bitcast_fusion = f32[512,1,128]{2,0,1:T(8,128)S(1)} fusion(bf16[4096,512]{1,0:T(8,128)(2,1)} %param.11, s32[]{:T(128)S(6)} %select_n.61, bf16[512,4096]{1,0:T(8,128)(2,1)} %param.8, f32[4096]{0:T(1024)S(1)} %convert_element_type.102, f32[512]{0:T(512)S(1)} %add_rsqrt_fusion), kind=kOutput, calls=%fused_computation.5 | convolution fusion | flops 545259520 | bytes 5523460 | tf_op jit(solution)/shard_map/dot_general | solution.py:159
  16.7 2.6 %convolution_convert_fusion = bf16[512,128]{1,0:T(8,128)(2,1)S(1)} fusion(bf16[4096,512]{1,0:T(8,128)(2,1)} %param.12, s32[]{:T(128)S(6)} %select_n.61, bf16[512,4096]{1,0:T(8,128)(2,1)S(1)} %copy-done, f32[4096]{0:T(1024)S(1)} %convert_element_type.102, f32[512]{0:T(512)S(1)} %add_rsqrt_fusion), kind=kOutput, calls=%fused_computation.6 | convolution fusion | flops 545325056 | bytes 5392388 | tf_op jit(solution)/shard_map/dot_general | solution.py:161
  19.2 1.2 fusion.10
  20.5 0.1 maximum_bitcast_fusion
  20.6 0.7 pad_maximum_fusion.2
  21.3 0.1 reshape.280
  21.4 0.1 reshape_squeeze.19
  21.5 0.1 reshape_squeeze.20
  21.6 0.6 fusion.24
  27.4 0.1 reshape_squeeze.22
  27.5 0.1 reshape_squeeze.23
  27.5 0.7 fusion.22
  33.4 0.1 broadcast_in_dim_reshape_squeeze.13
  33.5 0.1 broadcast_in_dim_reshape_squeeze.15
  33.5 6.0 %fusion.17 = f32[512,512]{0,1:T(8,128)S(1)} fusion(bf16[4096,512]{1,0:T(8,128)(2,1)} %param.10, bf16[512,4096]{1,0:T(8,128)(2,1)} %param.8, f32[4096]{0:T(1024)S(1)} %convert_element_type.102, f32[512]{0:T(512)S(1)} %add_rsqrt_fusion), kind=kOutput, calls=%fused_computation.46 | convolution fusion | flops 2155872256 | bytes 9455616 | tf_op jit(solution)/shard_map/dot_general | solution.py:168
  39.6 0.1 fusion.19
  39.7 0.4 copy.43
  40.1 0.4 copy.44
  40.5 1.0 multiply_cosine_fusion.1
  41.5 0.6 subtract_convert_fusion
  42.1 0.7 pad_maximum_fusion
  42.8 0.2 convert_element_type.105
  43.0 0.1 broadcast_in_dim_reshape_squeeze.12
  43.1 0.1 broadcast_in_dim_reshape_squeeze.14
  43.2 0.8 fusion.20
  44.0 0.8 copy.37.start_ref
  44.8 0.8 copy.38.index_ref
  45.6 14.2 %all-gather.2.cloned.1.call-done.kv_ref = bf16[8192,256]{1,0:T(8,128)(2,1)} async-done(((bf16[512,256]{1,0:T(8,128)(2,1)}), bf16[8192,256]{1,0:T(8,128)(2,1)}) %all-gather.2.cloned.1.call-update) | async-done | bytes 4194320 | tf_op jit(solution)/shard_map/all_gather | solution.py:165
  59.8 20.8 %shard_map.95 = bf16[256,4096]{1,0:T(8,128)(2,1)} custom-call(s32[1]{0:T(128)S(6)} %select_n.56.lo_ref, s32[1]{0:T(128)S(6)} %select_n.57.hi_ref, s32[1]{0:T(128)} %get-tuple-element.18.base_ref, s32[1]{0:T(128)} %get-tuple-element.19.last_start_ref, bf16[256,512]{1,0:T(8,128)(2,1)} %bitcast.38, s32[256,1]{1,0:T(8,128)} %copy.37.start_ref, ...), custom_call_target="tpu_custom_call" | custom-call | tf_op jit(solution)/shard_map/pallas_call | solution.py:135
  80.6 5.9 %all-to-all-start = ((bf16[8,32,4096]{2,1,0:T(8,128)(2,1)}), bf16[8,32,4096]{2,1,0:T(8,128)(2,1)S(1)}, u32[]{:S(2)}, u32[]{:S(2)}) async-start(bf16[8,32,4096]{2,1,0:T(8,128)(2,1)} %bitcast.35), calls=%async_computation | async-start | bytes 4194304 | tf_op jit(solution)/shard_map/all_to_all | solution.py:189
  86.5 0.8 copy.39.start_ref
  87.3 0.8 copy.40.index_ref
  88.1 20.7 %shard_map.96 = bf16[256,4096]{1,0:T(8,128)(2,1)} custom-call(s32[1]{0:T(128)S(6)} %select_n.58.lo_ref, s32[1]{0:T(128)S(6)} %select_n.59.hi_ref, s32[1]{0:T(128)} %get-tuple-element.25.base_ref, s32[1]{0:T(128)} %get-tuple-element.26.last_start_ref, bf16[256,512]{1,0:T(8,128)(2,1)} %bitcast.37, s32[256,1]{1,0:T(8,128)} %copy.39.start_ref, ...), custom_call_target="tpu_custom_call" | custom-call | tf_op jit(solution)/shard_map/pallas_call | solution.py:135
  108.8 6.6 %all-to-all-done = bf16[8,32,4096]{2,1,0:T(8,128)(2,1)S(1)} async-done(((bf16[8,32,4096]{2,1,0:T(8,128)(2,1)}), bf16[8,32,4096]{2,1,0:T(8,128)(2,1)S(1)}, u32[]{:S(2)}, u32[]{:S(2)}) %all-to-all-start) | async-done | bytes 2097184 | tf_op jit(solution)/shard_map/all_to_all | solution.py:189
  115.4 4.4 %all-to-all-start.1 = ((bf16[8,32,4096]{2,1,0:T(8,128)(2,1)}), bf16[8,32,4096]{2,1,0:T(8,128)(2,1)}, u32[]{:S(2)}, u32[]{:S(2)}) async-start(bf16[8,32,4096]{2,1,0:T(8,128)(2,1)} %bitcast.34), calls=%async_computation.1 | async-start | bytes 4194304 | tf_op jit(solution)/shard_map/all_to_all | solution.py:189
  119.7 0.2 select_reduce_fusion.1
  119.9 0.6 fusion.26
  123.0 0.8 dynamic-slice_bitcast_fusion.3
  123.8 0.7 pad_maximum_fusion.3
  124.5 0.3 add_convert_fusion.2
  124.8 22.9 %all-to-all-done.1 = bf16[8,32,4096]{2,1,0:T(8,128)(2,1)} async-done(((bf16[8,32,4096]{2,1,0:T(8,128)(2,1)}), bf16[8,32,4096]{2,1,0:T(8,128)(2,1)}, u32[]{:S(2)}, u32[]{:S(2)}) %all-to-all-start.1) | async-done | bytes 2097184 | tf_op jit(solution)/shard_map/all_to_all | solution.py:189
  147.7 1.8 %add_convert_fusion.1 = bf16[1,32,4096]{2,1,0:T(8,128)(2,1)S(1)} fusion(bf16[8,32,4096]{2,1,0:T(8,128)(2,1)} %all-to-all-done.1), kind=kLoop, calls=%fused_computation.13 | loop fusion | flops 2097152 | bytes 2359296 | tf_op jit(solution)/shard_map/convert_element_type | solution.py:195
  149.5 0.8 pad_maximum_fusion.1
  (15 shorter events, 0.2 us)
Async XLA Ops:
  7.2 52.6 %all-gather.2.cloned.1.call-start = ((), (), s32[]{:S(2)}) async-start(), calls=%async_computation.2 | async-start | bytes 4456448 | tf_op jit(solution)/shard_map/all_gather | solution.py:165
  12.7 4.0 %copy-start = (bf16[512,4096]{1,0:T(8,128)(2,1)S(1)}, bf16[512,4096]{1,0:T(8,128)(2,1)}, u32[]{:S(2)}) copy-start(bf16[512,4096]{1,0:T(8,128)(2,1)} %param.8) | copy-start | bytes 12582916
  80.6 34.8 %all-to-all-start = ((bf16[8,32,4096]{2,1,0:T(8,128)(2,1)}), bf16[8,32,4096]{2,1,0:T(8,128)(2,1)S(1)}, u32[]{:S(2)}, u32[]{:S(2)}) async-start(bf16[8,32,4096]{2,1,0:T(8,128)(2,1)} %bitcast.35), calls=%async_computation | async-start | bytes 4194304 | tf_op jit(solution)/shard_map/all_to_all | solution.py:189
  108.8 11.0 %copy-start.1 = (s32[64]{0:T(128)S(1)}, s32[64]{0:T(128)}, u32[]{:S(2)}) copy-start(s32[64]{0:T(128)} %param.15) | copy-start | bytes 772
  115.4 32.4 %all-to-all-start.1 = ((bf16[8,32,4096]{2,1,0:T(8,128)(2,1)}), bf16[8,32,4096]{2,1,0:T(8,128)(2,1)}, u32[]{:S(2)}, u32[]{:S(2)}) async-start(bf16[8,32,4096]{2,1,0:T(8,128)(2,1)} %bitcast.34), calls=%async_computation.1 | async-start | bytes 4194304 | tf_op jit(solution)/shard_map/all_to_all | solution.py:189
Sparse Core Ops, SparseCore 0:
  21.4 38.2 all-gather.1

commit v4 on v3

--- a/solution.py
+++ b/solution.py
@@ -155,12 +155,13 @@
 
     key_columns = lax.dynamic_slice_in_dim(w_key, kv_head * HD, HD, 1)
     value_columns = lax.dynamic_slice_in_dim(w_value, kv_head * HD, HD, 1)
-    keys_here = rotate(
-        jnp.dot(normed, key_columns, preferred_element_type=jnp.float32)[:, None, :], position
-    )[:, 0].astype(jnp.bfloat16)
-    values_here = jnp.dot(normed, value_columns, preferred_element_type=jnp.float32).astype(
-        jnp.bfloat16
-    )
+    projected = jnp.dot(
+        normed,
+        jnp.concatenate([key_columns, value_columns], axis=1),
+        preferred_element_type=jnp.float32,
+    )
+    keys_here = rotate(projected[:, None, :HD], position)[:, 0].astype(jnp.bfloat16)
+    values_here = projected[:, HD:].astype(jnp.bfloat16)
     keys_values = jnp.concatenate([keys_here, values_here], axis=1)
     gathered = lax.all_gather(keys_values, "seq", axis=0, tiled=True)
 

time: 160 us -> 154 us (0.963)
  the two profiles are of different devices: /device:TPU:18 before, /device:TPU:24 now
where the time goes in v4:
time: 154 us; the launch traced here: 152 us
  waiting for transfers between devices  46.5 us (30%)
  Pallas kernels  36.7 us (24%)
  between operations  27.1 us (18%)
  other arithmetic  12.2 us (8%)
  local copies, waits for them, and re-layouts  11.5 us (7%)
  starting transfers between devices  10.9 us (7%)
  matrix products  7.26 us (5%)
    pallas_call x2, Pallas kernels, flash_attention(): pl.pallas_call(flash_kernel, grid_spec=grid_spec, out_shape=jax.ShapeDtyp...  36.7 us
    all_to_all x2, waiting for transfers between devices, on_device(): lax.all_to_all(partial_out, ('tpz', 'tpx'), split_axis=0, concat_axis=0,...  32 us
    all_gather x1, waiting for transfers between devices, on_device(): gathered = lax.all_gather(keys_values, 'seq', axis=0, tiled=True)  14.5 us
    all_to_all x2, starting transfers between devices, on_device(): lax.all_to_all(partial_out, ('tpz', 'tpx'), split_axis=0, concat_axis=0,...  10.9 us
    dot_general x1, matrix products, on_device(): jnp.dot(normed, w_query, preferred_element_type=jnp.float32)  5.93 us
    optimization_barrier x4, local copies, waits for them, and re-layouts, on_device(): chunk_inputs = lax.optimization_barrier(chunk_inputs)  3.19 us
    reduce_sum x1, other arithmetic, normalize(): jnp.mean(hidden * hidden, axis=-1, keepdims=True) + epsilon  3.08 us
  transfers between devices with their start and end apart: 3, of which 3 were waited for; matrix products, arithmetic and copies ran while one was open for 12% of the time, Pallas kernels for 12%

profile of v4, /device:TPU:24, one launch (start us, length us, event | category | flops | bytes accessed | tf_op | source)
XLA Modules:
  0.0 152.2 jit_solution(9316212060667775401)
XLA Ops:
  7.2 0.7 convert_element_type.100
  7.9 3.1 %fusion = f32[512]{0:T(512)S(1)} fusion(bf16[512,4096]{1,0:T(8,128)(2,1)} %param.8), kind=kLoop, calls=%fused_computation.2 | loop fusion | flops 6290944 | bytes 4196352 | tf_op jit(solution)/shard_map/reduce_sum | solution.py:43
  11.1 1.8 %constant_dynamic-slice_fusion = (bf16[4096,128]{1,0:T(8,128)(2,1)S(1)}, bf16[4096,128]{1,0:T(8,128)(2,1)S(1)}) fusion(bf16[4096,512]{1,0:T(8,128)(2,1)} %param.12, s32[]{:T(128)S(6)} %select_n.61, bf16[4096,512]{1,0:T(8,128)(2,1)} %param.11), kind=kLoop, calls=%fused_computation.45 | loop fusion | bytes 4194308 | tf_op jit(solution)/shard_map/dynamic_slice | solution.py:157
  12.9 1.0 copy-done
  13.9 1.3 fusion.3
  15.3 0.1 copy.32
  15.4 0.1 reduce
  15.6 0.1 select_reduce_fusion
  15.7 1.2 fusion.15
  16.9 0.1 maximum_bitcast_fusion
  17.0 0.7 pad_maximum_fusion.2
  17.7 0.1 reshape.280
  17.9 0.1 broadcast_in_dim_reshape_squeeze.13
  17.9 0.1 reshape_squeeze.20
  18.0 0.1 reshape_squeeze.19
  18.1 0.6 fusion.24
  23.9 0.1 broadcast_in_dim_reshape_squeeze.15
  24.1 0.1 reshape_squeeze.22
  24.1 0.6 fusion.22
  29.9 5.9 %fusion.8 = f32[512,512]{0,1:T(8,128)S(1)} fusion(bf16[4096,512]{1,0:T(8,128)(2,1)} %param.10, bf16[512,4096]{1,0:T(8,128)(2,1)} %param.8, f32[4096]{0:T(1024)S(1)} %convert_element_type.100, f32[512]{0:T(512)S(1)} %add_rsqrt_fusion), kind=kOutput, calls=%fused_computation.9 | convolution fusion | flops 2155872256 | bytes 9455616 | tf_op jit(solution)/shard_map/dot_general | solution.py:169
  35.9 0.1 fusion.19
  36.0 0.4 copy.43
  36.4 0.4 copy.42
  36.8 1.0 multiply_cosine_fusion.1
  37.8 0.6 subtract_convert_fusion
  38.4 0.7 pad_maximum_fusion
  39.1 0.2 convert_element_type.103
  39.3 0.1 broadcast_in_dim_reshape_squeeze.12
  39.4 0.1 broadcast_in_dim_reshape_squeeze.14
  39.5 0.9 fusion.20
  40.3 0.8 copy.39.start_ref
  41.1 0.8 copy.40.index_ref
  41.9 14.5 %all-gather.2.cloned.1.call-done.kv_ref = bf16[8192,256]{1,0:T(8,128)(2,1)} async-done(((bf16[512,256]{1,0:T(8,128)(2,1)}), bf16[8192,256]{1,0:T(8,128)(2,1)}) %all-gather.2.cloned.1.call-update) | async-done | bytes 4194320 | tf_op jit(solution)/shard_map/all_gather | solution.py:166
  56.4 18.5 %shard_map.96 = bf16[256,4096]{1,0:T(8,128)(2,1)} custom-call(s32[1]{0:T(128)S(6)} %select_n.58.lo_ref, s32[1]{0:T(128)S(6)} %select_n.59.hi_ref, s32[1]{0:T(128)} %get-tuple-element.25.base_ref, s32[1]{0:T(128)} %get-tuple-element.26.last_start_ref, bf16[256,512]{1,0:T(8,128)(2,1)} %bitcast.38, s32[256,1]{1,0:T(8,128)} %copy.39.start_ref, ...), custom_call_target="tpu_custom_call" | custom-call | tf_op jit(solution)/shard_map/pallas_call | solution.py:135
  74.9 6.5 %all-to-all-start.1 = ((bf16[8,32,4096]{2,1,0:T(8,128)(2,1)}), bf16[8,32,4096]{2,1,0:T(8,128)(2,1)S(1)}, u32[]{:S(2)}, u32[]{:S(2)}) async-start(bf16[8,32,4096]{2,1,0:T(8,128)(2,1)} %bitcast.35), calls=%async_computation.1 | async-start | bytes 4194304 | tf_op jit(solution)/shard_map/all_to_all | solution.py:190
  81.4 0.8 copy.37.start_ref
  82.2 0.8 copy.38.index_ref
  83.0 18.2 %shard_map.95 = bf16[256,4096]{1,0:T(8,128)(2,1)} custom-call(s32[1]{0:T(128)S(6)} %select_n.56.lo_ref, s32[1]{0:T(128)S(6)} %select_n.57.hi_ref, s32[1]{0:T(128)} %get-tuple-element.18.base_ref, s32[1]{0:T(128)} %get-tuple-element.19.last_start_ref, bf16[256,512]{1,0:T(8,128)(2,1)} %bitcast.37, s32[256,1]{1,0:T(8,128)} %copy.37.start_ref, ...), custom_call_target="tpu_custom_call" | custom-call | tf_op jit(solution)/shard_map/pallas_call | solution.py:135
  101.3 9.0 %all-to-all-done.1 = bf16[8,32,4096]{2,1,0:T(8,128)(2,1)S(1)} async-done(((bf16[8,32,4096]{2,1,0:T(8,128)(2,1)}), bf16[8,32,4096]{2,1,0:T(8,128)(2,1)S(1)}, u32[]{:S(2)}, u32[]{:S(2)}) %all-to-all-start.1) | async-done | bytes 2097184 | tf_op jit(solution)/shard_map/all_to_all | solution.py:190
  110.3 4.4 %all-to-all-start = ((bf16[8,32,4096]{2,1,0:T(8,128)(2,1)}), bf16[8,32,4096]{2,1,0:T(8,128)(2,1)}, u32[]{:S(2)}, u32[]{:S(2)}) async-start(bf16[8,32,4096]{2,1,0:T(8,128)(2,1)} %bitcast.34), calls=%async_computation | async-start | bytes 4194304 | tf_op jit(solution)/shard_map/all_to_all | solution.py:190
  114.7 0.2 select_reduce_fusion.1
  114.9 0.6 fusion.26
  117.9 0.8 dynamic-slice_bitcast_fusion.3
  118.8 0.7 pad_maximum_fusion.3
  119.5 0.3 add_convert_fusion.1
  119.7 23.0 %all-to-all-done = bf16[8,32,4096]{2,1,0:T(8,128)(2,1)} async-done(((bf16[8,32,4096]{2,1,0:T(8,128)(2,1)}), bf16[8,32,4096]{2,1,0:T(8,128)(2,1)}, u32[]{:S(2)}, u32[]{:S(2)}) %all-to-all-start) | async-done | bytes 2097184 | tf_op jit(solution)/shard_map/all_to_all | solution.py:190
  142.7 1.8 %add_convert_fusion.2 = bf16[1,32,4096]{2,1,0:T(8,128)(2,1)S(1)} fusion(bf16[8,32,4096]{2,1,0:T(8,128)(2,1)} %all-to-all-done), kind=kLoop, calls=%fused_computation.15 | loop fusion | flops 2097152 | bytes 2359296 | tf_op jit(solution)/shard_map/convert_element_type | solution.py:196
  144.5 0.8 pad_maximum_fusion.1
  (19 shorter events, 0.3 us)
Async XLA Ops:
  7.2 49.2 %all-gather.2.cloned.1.call-start = ((), (), s32[]{:S(2)}) async-start(), calls=%async_computation.2 | async-start | bytes 4456448 | tf_op jit(solution)/shard_map/all_gather | solution.py:166
  11.0 2.9 %copy-start = (bf16[512,4096]{1,0:T(8,128)(2,1)S(1)}, bf16[512,4096]{1,0:T(8,128)(2,1)}, u32[]{:S(2)}) copy-start(bf16[512,4096]{1,0:T(8,128)(2,1)} %param.8) | copy-start | bytes 12582916
  13.9 1.4 copy-start.1
  74.9 35.4 %all-to-all-start.1 = ((bf16[8,32,4096]{2,1,0:T(8,128)(2,1)}), bf16[8,32,4096]{2,1,0:T(8,128)(2,1)S(1)}, u32[]{:S(2)}, u32[]{:S(2)}) async-start(bf16[8,32,4096]{2,1,0:T(8,128)(2,1)} %bitcast.35), calls=%async_computation.1 | async-start | bytes 4194304 | tf_op jit(solution)/shard_map/all_to_all | solution.py:190
  101.3 13.4 %copy-start.2 = (s32[64]{0:T(128)S(1)}, s32[64]{0:T(128)}, u32[]{:S(2)}) copy-start(s32[64]{0:T(128)} %param.15) | copy-start | bytes 772
  110.3 32.4 %all-to-all-start = ((bf16[8,32,4096]{2,1,0:T(8,128)(2,1)}), bf16[8,32,4096]{2,1,0:T(8,128)(2,1)}, u32[]{:S(2)}, u32[]{:S(2)}) async-start(bf16[8,32,4096]{2,1,0:T(8,128)(2,1)} %bitcast.34), calls=%async_computation | async-start | bytes 4194304 | tf_op jit(solution)/shard_map/all_to_all | solution.py:190
Sparse Core Ops, SparseCore 0:
  17.9 38.4 all-gather.1

commit v5 on v4

--- a/solution.py
+++ b/solution.py
@@ -47,8 +47,8 @@
 def flash_kernel(lo_ref, hi_ref, base_ref, last_start_ref, q_ref, start_ref, index_ref, kv_ref, w_ref, o_ref):
     i = pl.program_id(0)
     heads = q_ref.shape[1] // HD
-    row_index = index_ref[...]
-    row_start = start_ref[...]
+    row_index = index_ref[:, 0:1]
+    row_start = start_ref[:, 0:1]
     scale = HD ** (-0.5)
 
     def step(kb, carry, masked):
@@ -125,8 +125,8 @@
         grid=(q_blocks,),
         in_specs=[
             pl.BlockSpec((BQ, width), rows_of),
-            pl.BlockSpec((BQ, 1), rows_of),
-            pl.BlockSpec((BQ, 1), rows_of),
+            pl.BlockSpec((BQ, HD), rows_of),
+            pl.BlockSpec((BQ, HD), rows_of),
             pl.BlockSpec((kv_rows, 2 * HD), lambda i, *_: (0, 0)),
             pl.BlockSpec((width, model_width), lambda i, *_: (0, 0)),
         ],
@@ -182,7 +182,8 @@
         s_rows = chunk_start[:, c].reshape(tp_count * piece)
         i_rows = chunk_index[:, c].reshape(tp_count * piece)
         bounds = (s_rows[:1] // BK, i_rows[-1:] // BK, i_rows[:1], s_rows[-1:])
-        chunk_inputs.append((q_rows, s_rows[:, None], i_rows[:, None], bounds))
+        lanes = lambda v: jnp.broadcast_to(v[:, None], (v.shape[0], HD))
+        chunk_inputs.append((q_rows, lanes(s_rows), lanes(i_rows), bounds))
     chunk_inputs = lax.optimization_barrier(chunk_inputs)
     outputs = []
     for q_rows, s_rows, i_rows, bounds in chunk_inputs:

time: 154 us -> 155 us (level)
  Pallas kernels: 36.7 us -> 41.5 us
  waiting for transfers between devices: 46.5 us -> 43.2 us
    pallas_call x2, Pallas kernels: 36.7 us -> 41.5 us  [flash_attention(): pl.pallas_call(flash_kernel, grid_spec=grid_spec, out_shape=jax.ShapeDtyp...]
    broadcast_in_dim x0 -> x8, local copies, waits for them, and re-layouts: none -> 3.3 us  [on_device(): lanes = lambda v: jnp.broadcast_to(v[:, None], (v.shape[0], HD))]
    optimization_barrier x4 -> x0, local copies, waits for them, and re-layouts: 3.19 us -> none  [on_device(): chunk_inputs = lax.optimization_barrier(chunk_inputs)]
    all_gather x1, waiting for transfers between devices: 14.5 us -> 12 us  [on_device(): gathered = lax.all_gather(keys_values, 'seq', axis=0, tiled=True)]
  transfers between devices with their start and end apart: 3 -> 3, of which waited for: 3 -> 3; matrix products, arithmetic and copies ran while one was open for 12% -> 12% of each run, Pallas kernels for 12% -> 13%
where the time goes in v5:
time: 155 us
  waiting for transfers between devices  43.2 us (28%)
  Pallas kernels  41.5 us (27%)
  between operations  27.2 us (18%)
  other arithmetic  12.2 us (8%)
  local copies, waits for them, and re-layouts  12.1 us (8%)
  starting transfers between devices  11 us (7%)
  matrix products  7.34 us (5%)
    pallas_call x2, Pallas kernels, flash_attention(): pl.pallas_call(flash_kernel, grid_spec=grid_spec, out_shape=jax.ShapeDtyp...  41.5 us
    all_to_all x2, waiting for transfers between devices, on_device(): lax.all_to_all(partial_out, ('tpz', 'tpx'), split_axis=0, concat_axis=0,...  31.2 us
    all_gather x1, waiting for transfers between devices, on_device(): gathered = lax.all_gather(keys_values, 'seq', axis=0, tiled=True)  12 us
    all_to_all x2, starting transfers between devices, on_device(): lax.all_to_all(partial_out, ('tpz', 'tpx'), split_axis=0, concat_axis=0,...  11 us
    dot_general x1, matrix products, on_device(): jnp.dot(normed, w_query, preferred_element_type=jnp.float32)  6.02 us
    broadcast_in_dim x8, local copies, waits for them, and re-layouts, on_device(): lanes = lambda v: jnp.broadcast_to(v[:, None], (v.shape[0], HD))  3.3 us
  transfers between devices with their start and end apart: 3, of which 3 were waited for; matrix products, arithmetic and copies ran while one was open for 12% of the time, Pallas kernels for 13%

profile of v5, /device:TPU:24, one launch (start us, length us, event | category | flops | bytes accessed | tf_op | source)
XLA Modules:
  0.0 154.5 jit_solution(16783260121381727827)
XLA Ops:
  7.2 0.0 all-gather.2.cloned.1.call-start
  7.2 0.7 convert_element_type.100
  7.9 3.1 %fusion = f32[512]{0:T(512)S(1)} fusion(bf16[512,4096]{1,0:T(8,128)(2,1)} %param.8), kind=kLoop, calls=%fused_computation.2 | loop fusion | flops 6290944 | bytes 4196352 | tf_op jit(solution)/shard_map/reduce_sum | solution.py:43
  11.1 1.8 %constant_dynamic-slice_fusion = (bf16[4096,128]{1,0:T(8,128)(2,1)S(1)}, bf16[4096,128]{1,0:T(8,128)(2,1)S(1)}) fusion(bf16[4096,512]{1,0:T(8,128)(2,1)} %param.12, s32[]{:T(128)S(6)} %select_n.61, bf16[4096,512]{1,0:T(8,128)(2,1)} %param.11), kind=kLoop, calls=%fused_computation.49 | loop fusion | bytes 4194308 | tf_op jit(solution)/shard_map/dynamic_slice | solution.py:157
  12.9 1.0 copy-done
  13.9 1.3 fusion.3
  15.3 0.1 copy.24
  15.4 0.1 reduce
  15.6 0.1 select_reduce_fusion
  15.7 1.2 fusion.15
  16.9 0.1 maximum_bitcast_fusion
  17.0 0.7 pad_maximum_fusion.2
  17.7 0.1 reshape.284
  17.9 0.1 broadcast_in_dim.40
  18.0 0.6 fusion.23
  19.9 0.1 broadcast_in_dim.75
  20.6 0.6 fusion.24
  24.4 0.1 broadcast_in_dim.77
  24.5 0.6 fusion.21
  27.7 0.1 broadcast_in_dim.79
  27.8 0.6 fusion.22
  31.0 6.0 %fusion.8 = f32[512,512]{0,1:T(8,128)S(1)} fusion(bf16[4096,512]{1,0:T(8,128)(2,1)} %param.10, bf16[512,4096]{1,0:T(8,128)(2,1)} %param.8, f32[4096]{0:T(1024)S(1)} %convert_element_type.100, f32[512]{0:T(512)S(1)} %add_rsqrt_fusion), kind=kOutput, calls=%fused_computation.9 | convolution fusion | flops 2155872256 | bytes 9455616 | tf_op jit(solution)/shard_map/dot_general | solution.py:169
  37.0 0.1 fusion.19
  37.1 0.4 copy.31
  37.5 0.4 copy.30
  37.9 1.0 multiply_cosine_fusion.1
  38.9 0.6 subtract_convert_fusion
  39.5 0.7 pad_maximum_fusion
  40.2 0.2 convert_element_type.103
  40.5 0.8 fusion.20
  41.4 0.7 broadcast_in_dim.74.start_ref
  42.1 0.7 broadcast_in_dim.76.index_ref
  42.8 0.8 broadcast_in_dim.78.start_ref
  43.6 0.7 broadcast_in_dim.80.index_ref
  44.3 12.0 %all-gather.2.cloned.1.call-done.kv_ref = bf16[8192,256]{1,0:T(8,128)(2,1)} async-done(((bf16[512,256]{1,0:T(8,128)(2,1)}), bf16[8192,256]{1,0:T(8,128)(2,1)}) %all-gather.2.cloned.1.call-update) | async-done | bytes 4194320 | tf_op jit(solution)/shard_map/all_gather | solution.py:166
  56.4 20.8 %shard_map.96 = bf16[256,4096]{1,0:T(8,128)(2,1)} custom-call(s32[1]{0:T(128)S(6)} %select_n.58.lo_ref, s32[1]{0:T(128)S(6)} %select_n.59.hi_ref, s32[1]{0:T(128)} %get-tuple-element.25.base_ref, s32[1]{0:T(128)} %get-tuple-element.26.last_start_ref, bf16[256,512]{1,0:T(8,128)(2,1)} %bitcast.28, s32[256,128]{1,0:T(8,128)} %broadcast_in_dim.78.start_ref, ...), custom_call_target="tpu_custom_call" | custom-call | tf_op jit(solution)/shard_map/pallas_call | solution.py:135
  77.2 6.6 %all-to-all-start.1 = ((bf16[8,32,4096]{2,1,0:T(8,128)(2,1)}), bf16[8,32,4096]{2,1,0:T(8,128)(2,1)S(1)}, u32[]{:S(2)}, u32[]{:S(2)}) async-start(bf16[8,32,4096]{2,1,0:T(8,128)(2,1)} %bitcast.25), calls=%async_computation.1 | async-start | bytes 4194304 | tf_op jit(solution)/shard_map/all_to_all | solution.py:191
  83.8 20.7 %shard_map.95 = bf16[256,4096]{1,0:T(8,128)(2,1)} custom-call(s32[1]{0:T(128)S(6)} %select_n.56.lo_ref, s32[1]{0:T(128)S(6)} %select_n.57.hi_ref, s32[1]{0:T(128)} %get-tuple-element.18.base_ref, s32[1]{0:T(128)} %get-tuple-element.19.last_start_ref, bf16[256,512]{1,0:T(8,128)(2,1)} %bitcast.27, s32[256,128]{1,0:T(8,128)} %broadcast_in_dim.74.start_ref, ...), custom_call_target="tpu_custom_call" | custom-call | tf_op jit(solution)/shard_map/pallas_call | solution.py:135
  104.5 8.2 %all-to-all-done.1 = bf16[8,32,4096]{2,1,0:T(8,128)(2,1)S(1)} async-done(((bf16[8,32,4096]{2,1,0:T(8,128)(2,1)}), bf16[8,32,4096]{2,1,0:T(8,128)(2,1)S(1)}, u32[]{:S(2)}, u32[]{:S(2)}) %all-to-all-start.1) | async-done | bytes 2097184 | tf_op jit(solution)/shard_map/all_to_all | solution.py:191
  112.7 4.4 %all-to-all-start = ((bf16[8,32,4096]{2,1,0:T(8,128)(2,1)}), bf16[8,32,4096]{2,1,0:T(8,128)(2,1)}, u32[]{:S(2)}, u32[]{:S(2)}) async-start(bf16[8,32,4096]{2,1,0:T(8,128)(2,1)} %bitcast.24), calls=%async_computation | async-start | bytes 4194304 | tf_op jit(solution)/shard_map/all_to_all | solution.py:191
  117.1 0.2 select_reduce_fusion.1
  117.3 0.6 fusion.25
  120.4 0.8 dynamic-slice_bitcast_fusion.3
  121.2 0.7 pad_maximum_fusion.3
  121.9 0.3 add_convert_fusion.1
  122.2 22.9 %all-to-all-done = bf16[8,32,4096]{2,1,0:T(8,128)(2,1)} async-done(((bf16[8,32,4096]{2,1,0:T(8,128)(2,1)}), bf16[8,32,4096]{2,1,0:T(8,128)(2,1)}, u32[]{:S(2)}, u32[]{:S(2)}) %all-to-all-start) | async-done | bytes 2097184 | tf_op jit(solution)/shard_map/all_to_all | solution.py:191
  145.1 1.8 %add_convert_fusion.2 = bf16[1,32,4096]{2,1,0:T(8,128)(2,1)S(1)} fusion(bf16[8,32,4096]{2,1,0:T(8,128)(2,1)} %all-to-all-done), kind=kLoop, calls=%fused_computation.15 | loop fusion | flops 2097152 | bytes 2359296 | tf_op jit(solution)/shard_map/convert_element_type | solution.py:197
  146.9 0.8 pad_maximum_fusion.1
  (16 shorter events, 0.2 us)
Async XLA Ops:
  7.2 49.2 %all-gather.2.cloned.1.call-start = ((), (), s32[]{:S(2)}) async-start(), calls=%async_computation.2 | async-start | bytes 4456448 | tf_op jit(solution)/shard_map/all_gather | solution.py:166
  11.0 2.9 %copy-start = (bf16[512,4096]{1,0:T(8,128)(2,1)S(1)}, bf16[512,4096]{1,0:T(8,128)(2,1)}, u32[]{:S(2)}) copy-start(bf16[512,4096]{1,0:T(8,128)(2,1)} %param.8) | copy-start | bytes 12582916
  13.9 1.4 copy-start.1
  77.2 35.5 %all-to-all-start.1 = ((bf16[8,32,4096]{2,1,0:T(8,128)(2,1)}), bf16[8,32,4096]{2,1,0:T(8,128)(2,1)S(1)}, u32[]{:S(2)}, u32[]{:S(2)}) async-start(bf16[8,32,4096]{2,1,0:T(8,128)(2,1)} %bitcast.25), calls=%async_computation.1 | async-start | bytes 4194304 | tf_op jit(solution)/shard_map/all_to_all | solution.py:191
  104.5 12.6 %copy-start.2 = (s32[64]{0:T(128)S(1)}, s32[64]{0:T(128)}, u32[]{:S(2)}) copy-start(s32[64]{0:T(128)} %param.15) | copy-start | bytes 772
  112.7 32.4 %all-to-all-start = ((bf16[8,32,4096]{2,1,0:T(8,128)(2,1)}), bf16[8,32,4096]{2,1,0:T(8,128)(2,1)}, u32[]{:S(2)}, u32[]{:S(2)}) async-start(bf16[8,32,4096]{2,1,0:T(8,128)(2,1)} %bitcast.24), calls=%async_computation | async-start | bytes 4194304 | tf_op jit(solution)/shard_map/all_to_all | solution.py:191
Sparse Core Ops, SparseCore 0:
  17.9 38.4 all-gather.1
